TPU v7x, 32 devices: a whole 2x2x4 slice. The times are simulated.
32 devices in a mesh: row: 8 (over y, x, core), col: 4 (over z).
Axes of the slice: x: 2, y: 2, z: 4, core: 2. Of those that a mesh axis runs over, the one named last changes fastest.
Arguments:
- features: bfloat16 [6144, 256], P(('col', 'row')), may hold values from -6 to 6
- edge_tiles: bfloat16 [8, 4, 12, 256, 256], P('row', 'col'), may hold values from 0.006225586 to 0.0625
- tile_rows: int32 [8, 4, 12], P('row', 'col'), may hold values from 0 to 2, as said below
- tile_cols: int32 [8, 4, 12], P('row', 'col'), may hold values from 0 to 5
- tile_count: int32 [8, 4], P('row', 'col'), may hold values from 3 to 12, as said below
- weight: bfloat16 [256, 256], replicated, may hold values from -0.375 to 0.375
- cotangent: bfloat16 [6144, 256], P(('row', 'col')), may hold values from -6 to 6
Outputs:
- activated: bfloat16 [6144, 256], P(('row', 'col'))
- feature_grad: bfloat16 [6144, 256], P(('col', 'row'))
Inputs may be any that keep to these rules, and one draw needn't show every extreme that they name: Within one device the pairs (tile_rows, tile_cols) of all 12 slots are distinct. Slots at or past tile_count hold no edges of the graph.
All inputs are finite; a program needn't handle non-finite values.
Results may differ from a plain program's by a relative error of at most 0.006.
Values may be sent and summed in bfloat16 or wider, within the bound.
No kernel may reach another device: no remote copies, remote signals or barrier semaphores. Data moves between devices by JAX's collectives and lax.ppermute only.
A program may use at most 64 MiB of HBM per device.

v0:
```python
import jax
import jax.numpy as jnp
from jax import lax
from jax.sharding import PartitionSpec as P


def silu_slope(mixed):
    sigma = jax.nn.sigmoid(mixed)
    return sigma * (1.0 + mixed * (1.0 - sigma))


def dense_layer(summed, grad_rows, weight):
    aggregated = summed.astype(jnp.bfloat16)
    mixed = jnp.dot(aggregated, weight, preferred_element_type=jnp.float32)
    activated = jax.nn.silu(mixed).astype(jnp.bfloat16)
    scaled = (grad_rows.astype(jnp.float32) * silu_slope(mixed)).astype(jnp.bfloat16)
    pulled = jnp.dot(scaled, weight.T, preferred_element_type=jnp.float32).astype(jnp.bfloat16)
    return (activated, pulled)


def scatter_sum(partial, axis):
    n = lax.axis_size(axis)
    me = lax.axis_index(axis)
    chunks = partial.reshape(n, partial.shape[0] // n, partial.shape[1])
    sent = chunks.astype(jnp.bfloat16)
    total = lax.dynamic_index_in_dim(chunks, me, 0, keepdims=False)
    for shift in range(1, n):
        piece = lax.dynamic_index_in_dim(sent, (me + shift) % n, 0, keepdims=False)
        got = lax.ppermute(piece, axis, [(i, (i + shift) % n) for i in range(n)])
        total = total + got.astype(jnp.float32)
    return total


def gather_rows(rows, axis):
    n = lax.axis_size(axis)
    me = lax.axis_index(axis)
    out = jnp.zeros((n,) + rows.shape, rows.dtype)
    out = lax.dynamic_update_index_in_dim(out, rows, me, 0)
    for shift in range(1, n):
        got = lax.ppermute(rows, axis, [(i, (i + shift) % n) for i in range(n)])
        out = lax.dynamic_update_index_in_dim(out, got, (me - shift) % n, 0)
    return out.reshape(n * rows.shape[0], rows.shape[1])


def on_device(features, edge_tiles, tile_rows, tile_cols, tile_count, weight, cotangent):
    blocks = edge_tiles[0, 0]
    row_slots = tile_rows[0, 0]
    col_slots = tile_cols[0, 0]
    filled = tile_count[0, 0]
    slot_total = blocks.shape[0]
    tile_size = blocks.shape[1]
    feat_width = features.shape[1]
    own_rows = features.shape[0]
    row_tiles = own_rows * lax.axis_size("col") // tile_size
    col_tiles = own_rows * lax.axis_size("row") // tile_size
    occupied = (jnp.arange(slot_total, dtype=jnp.int32) < filled).astype(jnp.bfloat16)
    row_hot = (row_slots[None, :] == jnp.arange(row_tiles, dtype=jnp.int32)[:, None]).astype(
        jnp.bfloat16
    )
    col_hot = (col_slots[None, :] == jnp.arange(col_tiles, dtype=jnp.int32)[:, None]).astype(
        jnp.bfloat16
    )
    select = row_hot[:, None, :] * col_hot[None, :, :] * occupied[None, None, :]
    dense = jnp.einsum("tck,kij->ticj", select, blocks, preferred_element_type=jnp.float32)
    dense = dense.astype(jnp.bfloat16).reshape(row_tiles * tile_size, col_tiles * tile_size)
    gathered = lax.all_gather(features, "row", axis=0, tiled=True)
    partial_value = jnp.dot(dense, gathered, preferred_element_type=jnp.float32)
    own_sums = scatter_sum(partial_value, "col")
    activated, pulled_own = dense_layer(own_sums, cotangent, weight)
    pulled_block = gather_rows(pulled_own, "col")
    partial_grad = lax.dot_general(
        dense, pulled_block, (((0,), (0,)), ((), ())), preferred_element_type=jnp.float32
    )
    feature_grad = scatter_sum(partial_grad, "row").astype(jnp.bfloat16)
    return (activated, feature_grad)


def solution(mesh):
    return jax.shard_map(
        on_device,
        mesh=mesh,
        in_specs=(
            P(("col", "row"), None),
            P("row", "col", None, None, None),
            P("row", "col", None),
            P("row", "col", None),
            P("row", "col"),
            P(),
            P(("row", "col"), None),
        ),
        out_specs=(P(("row", "col"), None), P(("col", "row"), None)),
        check_vma=False,
    )
```

profile of v0, /device:TPU:0, one launch (start us, length us, event | category | flops | bytes accessed | tf_op | source)
XLA Modules:
  0.0 76.7 jit_solution(16350948291646581301)
XLA Ops:
  1.4 0.7 fusion.20
  2.0 0.7 fusion.24
  2.7 2.6 %convolution_convert_fusion = bf16[3,6,256,256]{3,1,2,0:T(8,128)(2,1)S(1)} fusion(bf16[12,256,256]{2,1,0:T(8,128)(2,1)} %bitcast.92, bf16[12]{0:T(256)(128)(2,1)S(1)} %compare_convert_fusion, bf16[6,12]{1,0:T(8,128)(2,1)S(1)} %fusion.20, bf16[3,12]{1,0:T(4,128)(2,1)S(1)} %fusion.24), kind=kOutput, calls=%fused_computation | convolution fusion | flops 29492496 | bytes 3932400 | tf_op jit(solution)/shard_map/tck,kij->ticj/dot_general | solution.py:64
  5.3 3.6 %dot_general.22 = bf16[4,192,1536]{2,1,0:T(8,128)(2,1)} reshape(bf16[3,256,6,256]{3,2,1,0:T(8,128)(2,1)S(1)} %bitcast.88) | data formatting | bytes 4718592 | tf_op jit(solution)/shard_map/dot_general | solution.py:67
  9.0 11.9 %all_gather.3 = bf16[1536,256]{1,0:T(8,128)(2,1)S(1)} all-gather(bf16[192,256]{1,0:T(8,128)(2,1)S(1)} %copy-done.1), channel_id=1, replica_groups=mesh['row'=8,'col'=4] {'row'}, dimensions={0}, use_global_device_ids=true | all-gather | bytes 884736 | tf_op jit(solution)/shard_map/all_gather | solution.py:66
  20.8 3.5 %fusion.26 = (bf16[4,192,256]{2,1,0:T(8,128)(2,1)}, f32[4,192,256]{2,1,0:T(8,128)}) fusion(bf16[4,192,1536]{2,1,0:T(8,128)(2,1)} %dot_general.22, bf16[1536,256]{1,0:T(8,128)(2,1)S(1)} %all_gather.3), kind=kOutput, calls=%fused_computation.49 | convolution fusion | flops 604176384 | bytes 4325376 | tf_op jit(solution)/shard_map/dot_general | solution.py:67
  24.3 1.6 %dynamic-slice_bitcast_fusion.9 = (bf16[192,256]{1,0:T(8,128)(2,1)S(1)}, bf16[192,256]{1,0:T(8,128)(2,1)}, bf16[192,256]{1,0:T(8,128)(2,1)S(1)}) fusion(bf16[4,192,256]{2,1,0:T(8,128)(2,1)} %get-tuple-element.12, s32[]{:T(128)S(6)} %select_n.108, s32[]{:T(128)S(6)} %select_n.112, s32[]{:T(128)S(6)} %select_n.110), kind=kLoop, calls=%fused_computation.35 | loop fusion | bytes 589836 | tf_op jit(solution)/shard_map/jit(dynamic_index_in_dim)/squeeze | solution.py:28
  25.9 3.6 %collective-permute-start.2 = (bf16[192,256]{1,0:T(8,128)(2,1)}, bf16[192,256]{1,0:T(8,128)(2,1)}, u32[]{:S(2)}, u32[]{:S(2)}) collective-permute-start(bf16[192,256]{1,0:T(8,128)(2,1)} %get-tuple-element.10), channel_id=1, source_target_pairs={{0,3},{1,0},{2,1},{3,2},{4,7},{5,4},{6,5},{7,6},{8,11},{9,8},{10,9... | collective-permute-start | bytes 294920 | tf_op jit(solution)/shard_map/ppermute | solution.py:29
  29.6 1.0 %collective-permute-start = (bf16[192,256]{1,0:T(8,128)(2,1)S(1)}, bf16[192,256]{1,0:T(8,128)(2,1)}, u32[]{:S(2)}, u32[]{:S(2)}) collective-permute-start(bf16[192,256]{1,0:T(8,128)(2,1)S(1)} %get-tuple-element.9), channel_id=1, source_target_pairs={{0,1},{1,2},{2,3},{3,0},{4,5},{5,6},{6,7},{7,4},{8,9},{9,10},{10,1... | collective-permute-start | bytes 294920 | tf_op jit(solution)/shard_map/ppermute | solution.py:29
  30.6 2.5 %collective-permute-done.2 = bf16[192,256]{1,0:T(8,128)(2,1)} collective-permute-done((bf16[192,256]{1,0:T(8,128)(2,1)}, bf16[192,256]{1,0:T(8,128)(2,1)}, u32[]{:S(2)}, u32[]{:S(2)}) %collective-permute-start.2) | collective-permute-done | bytes 98336 | tf_op jit(solution)/shard_map/ppermute | solution.py:29
  33.1 6.2 %collective-permute-done.1 = bf16[192,256]{1,0:T(8,128)(2,1)} collective-permute-done((bf16[192,256]{1,0:T(8,128)(2,1)S(1)}, bf16[192,256]{1,0:T(8,128)(2,1)}, u32[]{:S(2)}, u32[]{:S(2)}) %collective-permute-start.1) | collective-permute-done | bytes 98336 | tf_op jit(solution)/shard_map/ppermute | solution.py:29
  39.3 1.9 %multiply_convert_fusion.1 = (bf16[192,256]{1,0:T(8,128)(2,1)}, f32[192,256]{1,0:T(8,128)S(1)}) fusion(bf16[256,256]{1,0:T(8,128)(2,1)S(1)} %copy-done, bf16[192,256]{1,0:T(8,128)(2,1)} %collective-permute-done.2, bf16[192,256]{1,0:T(8,128)(2,1)} %collective-permute-done.1, bf16[192,256]{1,0:T(8,128)(2,1)} %collective-permute-done, ...), kind=kOutput, calls=%fused_computation.19 | convolution fusion | flops 25755648 | bytes 917508 | tf_op jit(solution)/shard_map/dot_general | solution.py:14
  41.2 0.8 %broadcast_in_dim.21 = bf16[4,192,256]{2,1,0:T(8,128)(2,1)} broadcast(bf16[]{:T(256)} %constant.130.clone.1), dimensions={} | broadcast | bytes 393218 | tf_op jit(solution)/shard_map/broadcast_in_dim | solution.py:37
  42.0 1.8 %bitcast_dynamic-update-slice_fusion.3 = (bf16[4,192,256]{2,1,0:T(8,128)(2,1)}, bf16[192,256]{1,0:T(8,128)(2,1)S(1)}) fusion(bf16[4,192,256]{2,1,0:T(8,128)(2,1)} %broadcast_in_dim.21, s32[]{:T(128)S(6)} %select_n.106, bf16[256,256]{1,0:T(8,128)(2,1)S(1)} %copy-done, f32[192,256]{1,0:T(8,128)S(1)} %get-tuple-element.15, bf16[192,256]{1,0:T(8,128)(2,1)} %param.13), kind=kOutput, calls=%fused_computation.25 | convolution fusion | flops 25706496 | bytes 622596 | tf_op jit(solution)/shard_map/dot_general | solution.py:17
  43.8 2.2 %copy.16 = bf16[96,8,6,256]{3,1,2,0:T(8,128)(2,1)} copy(bf16[96,8,6,256]{3,2,1,0:T(8,128)(2,1)S(1)} %bitcast.89) | data formatting | bytes 4718592
  46.0 2.8 %copy.14 = bf16[1536,768]{1,0:T(8,128)(2,1)S(1)} copy(bf16[1536,768]{0,1:T(8,128)(2,1)} %bitcast.91) | data formatting | bytes 4718592 | tf_op jit(solution)/shard_map/dot_general | solution.py:71
  48.9 2.2 %collective-permute-start.4 = (bf16[192,256]{1,0:T(8,128)(2,1)S(1)}, bf16[192,256]{1,0:T(8,128)(2,1)S(1)}, u32[]{:S(2)}, u32[]{:S(2)}) collective-permute-start(bf16[192,256]{1,0:T(8,128)(2,1)S(1)} %get-tuple-element.17), channel_id=1, source_target_pairs={{0,2},{1,3},{2,0},{3,1},{4,6},{5,7},{6,4},{7,5},{8,10},{9,11},{10,... | collective-permute-start | bytes 294920 | tf_op jit(solution)/shard_map/ppermute | solution.py:40
  51.1 2.7 %collective-permute-start.5 = (bf16[192,256]{1,0:T(8,128)(2,1)S(1)}, bf16[192,256]{1,0:T(8,128)(2,1)S(1)}, u32[]{:S(2)}, u32[]{:S(2)}) collective-permute-start(bf16[192,256]{1,0:T(8,128)(2,1)S(1)} %get-tuple-element.17), channel_id=1, source_target_pairs={{0,3},{1,0},{2,1},{3,2},{4,7},{5,4},{6,5},{7,6},{8,11},{9,8},{10,9... | collective-permute-start | bytes 294920 | tf_op jit(solution)/shard_map/ppermute | solution.py:40
  53.8 0.6 bitcast_dynamic-update-slice_fusion.2
  54.4 2.9 %collective-permute-done.4 = bf16[192,256]{1,0:T(8,128)(2,1)S(1)} collective-permute-done((bf16[192,256]{1,0:T(8,128)(2,1)S(1)}, bf16[192,256]{1,0:T(8,128)(2,1)S(1)}, u32[]{:S(2)}, u32[]{:S(2)}) %collective-permute-start.4) | collective-permute-done | bytes 98336 | tf_op jit(solution)/shard_map/ppermute | solution.py:40
  57.4 0.6 bitcast_dynamic-update-slice_fusion.1
  58.0 0.6 bitcast_dynamic-update-slice_fusion
  58.7 2.9 %fusion.27 = (bf16[8,192,256]{2,1,0:T(8,128)(2,1)S(1)}, f32[8,192,256]{2,1,0:T(8,128)}) fusion(bf16[8,192,768]{2,1,0:T(8,128)(2,1)S(1)} %bitcast.90, bf16[768,256,1]{1,0,2:T(8,128)(2,1)} %bitcast.20), kind=kOutput, calls=%fused_computation.50 | convolution fusion | flops 604372992 | bytes 5111808 | tf_op jit(solution)/shard_map/dot_general | solution.py:71
  61.7 1.5 %collective-permute-start.11 = (bf16[192,256]{1,0:T(8,128)(2,1)S(1)}, bf16[192,256]{1,0:T(8,128)(2,1)S(1)}, u32[]{:S(2)}, u32[]{:S(2)}) collective-permute-start(bf16[192,256]{1,0:T(8,128)(2,1)S(1)} %get-tuple-element.4), channel_id=1, source_target_pairs={{0,24},{4,28},{8,0},{12,4},{16,8},{20,12},{24,16},{28,20},{1,25},{... | collective-permute-start | bytes 294920 | tf_op jit(solution)/shard_map/ppermute | solution.py:29
  63.3 1.2 %collective-permute-start.10 = (bf16[192,256]{1,0:T(8,128)(2,1)S(1)}, bf16[192,256]{1,0:T(8,128)(2,1)S(1)}, u32[]{:S(2)}, u32[]{:S(2)}) collective-permute-start(bf16[192,256]{1,0:T(8,128)(2,1)S(1)} %get-tuple-element.5), channel_id=1, source_target_pairs={{0,20},{4,24},{8,28},{12,0},{16,4},{20,8},{24,12},{28,16},{1,21},{... | collective-permute-start | bytes 294920 | tf_op jit(solution)/shard_map/ppermute | solution.py:29
  64.5 0.5 collective-permute-start.9
  65.1 1.1 %collective-permute-start.8 = (bf16[192,256]{1,0:T(8,128)(2,1)S(1)}, bf16[192,256]{1,0:T(8,128)(2,1)S(1)}, u32[]{:S(2)}, u32[]{:S(2)}) collective-permute-start(bf16[192,256]{1,0:T(8,128)(2,1)S(1)} %get-tuple-element.7), channel_id=1, source_target_pairs={{0,12},{4,16},{8,20},{12,24},{16,28},{20,0},{24,4},{28,8},{1,13},{... | collective-permute-start | bytes 294920 | tf_op jit(solution)/shard_map/ppermute | solution.py:29
  66.2 1.5 %collective-permute-start.7 = (bf16[192,256]{1,0:T(8,128)(2,1)S(1)}, bf16[192,256]{1,0:T(8,128)(2,1)S(1)}, u32[]{:S(2)}, u32[]{:S(2)}) collective-permute-start(bf16[192,256]{1,0:T(8,128)(2,1)S(1)} %get-tuple-element.8), channel_id=1, source_target_pairs={{0,8},{4,12},{8,16},{12,20},{16,24},{20,28},{24,0},{28,4},{1,9},{5... | collective-permute-start | bytes 294920 | tf_op jit(solution)/shard_map/ppermute | solution.py:29
  67.7 1.2 %collective-permute-done.11 = bf16[192,256]{1,0:T(8,128)(2,1)S(1)} collective-permute-done((bf16[192,256]{1,0:T(8,128)(2,1)S(1)}, bf16[192,256]{1,0:T(8,128)(2,1)S(1)}, u32[]{:S(2)}, u32[]{:S(2)}) %collective-permute-start.11) | collective-permute-done | bytes 98336 | tf_op jit(solution)/shard_map/ppermute | solution.py:29
  69.0 5.4 %collective-permute-done.9 = bf16[192,256]{1,0:T(8,128)(2,1)S(1)} collective-permute-done((bf16[192,256]{1,0:T(8,128)(2,1)S(1)}, bf16[192,256]{1,0:T(8,128)(2,1)S(1)}, u32[]{:S(2)}, u32[]{:S(2)}) %collective-permute-start.9) | collective-permute-done | bytes 98336 | tf_op jit(solution)/shard_map/ppermute | solution.py:29
  74.4 0.6 collective-permute-done.8
  75.0 1.7 %fusion.10 = bf16[192,256]{1,0:T(8,128)(2,1)} fusion(bf16[192,256]{1,0:T(8,128)(2,1)S(1)} %collective-permute-done.12, bf16[192,256]{1,0:T(8,128)(2,1)S(1)} %collective-permute-done.11, bf16[192,256]{1,0:T(8,128)(2,1)S(1)} %collective-permute-done.10, bf16[192,256]{1,0:T(8,128)(2,1)S(1)} %collective-permute-done.9, ...), kind=kLoop, calls=%fused_computation.13 | loop fusion | flops 737280 | bytes 983044 | tf_op jit(solution)/shard_map/convert_element_type | solution.py:74
  (17 shorter events, 0.2 us)
Async XLA Ops:
  0.6 38.7 %copy-start = (bf16[256,256]{1,0:T(8,128)(2,1)S(1)}, bf16[256,256]{1,0:T(8,128)(2,1)}, u32[]{:S(2)}) copy-start(bf16[256,256]{1,0:T(8,128)(2,1)} %param.12) | copy-start | bytes 393220
  5.3 3.6 %copy-start.1 = (bf16[192,256]{1,0:T(8,128)(2,1)S(1)}, bf16[192,256]{1,0:T(8,128)(2,1)}, u32[]{:S(2)}) copy-start(bf16[192,256]{1,0:T(8,128)(2,1)} %param.7) | copy-start | bytes 294916
  25.9 7.2 %collective-permute-start.2 = (bf16[192,256]{1,0:T(8,128)(2,1)}, bf16[192,256]{1,0:T(8,128)(2,1)}, u32[]{:S(2)}, u32[]{:S(2)}) collective-permute-start(bf16[192,256]{1,0:T(8,128)(2,1)} %get-tuple-element.10), channel_id=1, source_target_pairs={{0,3},{1,0},{2,1},{3,2},{4,7},{5,4},{6,5},{7,6},{8,11},{9,8},{10,9... | collective-permute-start | bytes 294920 | tf_op jit(solution)/shard_map/ppermute | solution.py:29
  29.5 9.7 %collective-permute-start.1 = (bf16[192,256]{1,0:T(8,128)(2,1)S(1)}, bf16[192,256]{1,0:T(8,128)(2,1)}, u32[]{:S(2)}, u32[]{:S(2)}) collective-permute-start(bf16[192,256]{1,0:T(8,128)(2,1)S(1)} %get-tuple-element.11), channel_id=1, source_target_pairs={{0,2},{1,3},{2,0},{3,1},{4,6},{5,7},{6,4},{7,5},{8,10},{9,11},{10,... | collective-permute-start | bytes 294920 | tf_op jit(solution)/shard_map/ppermute | solution.py:29
  29.6 9.7 %collective-permute-start = (bf16[192,256]{1,0:T(8,128)(2,1)S(1)}, bf16[192,256]{1,0:T(8,128)(2,1)}, u32[]{:S(2)}, u32[]{:S(2)}) collective-permute-start(bf16[192,256]{1,0:T(8,128)(2,1)S(1)} %get-tuple-element.9), channel_id=1, source_target_pairs={{0,1},{1,2},{2,3},{3,0},{4,5},{5,6},{6,7},{7,4},{8,9},{9,10},{10,1... | collective-permute-start | bytes 294920 | tf_op jit(solution)/shard_map/ppermute | solution.py:29
  43.8 10.0 %collective-permute-start.3 = (bf16[192,256]{1,0:T(8,128)(2,1)S(1)}, bf16[192,256]{1,0:T(8,128)(2,1)S(1)}, u32[]{:S(2)}, u32[]{:S(2)}) collective-permute-start(bf16[192,256]{1,0:T(8,128)(2,1)S(1)} %get-tuple-element.17), channel_id=1, source_target_pairs={{0,1},{1,2},{2,3},{3,0},{4,5},{5,6},{6,7},{7,4},{8,9},{9,10},{10,1... | collective-permute-start | bytes 294920 | tf_op jit(solution)/shard_map/ppermute | solution.py:40
  48.9 8.5 %collective-permute-start.4 = (bf16[192,256]{1,0:T(8,128)(2,1)S(1)}, bf16[192,256]{1,0:T(8,128)(2,1)S(1)}, u32[]{:S(2)}, u32[]{:S(2)}) collective-permute-start(bf16[192,256]{1,0:T(8,128)(2,1)S(1)} %get-tuple-element.17), channel_id=1, source_target_pairs={{0,2},{1,3},{2,0},{3,1},{4,6},{5,7},{6,4},{7,5},{8,10},{9,11},{10,... | collective-permute-start | bytes 294920 | tf_op jit(solution)/shard_map/ppermute | solution.py:40
  51.1 6.9 %collective-permute-start.5 = (bf16[192,256]{1,0:T(8,128)(2,1)S(1)}, bf16[192,256]{1,0:T(8,128)(2,1)S(1)}, u32[]{:S(2)}, u32[]{:S(2)}) collective-permute-start(bf16[192,256]{1,0:T(8,128)(2,1)S(1)} %get-tuple-element.17), channel_id=1, source_target_pairs={{0,3},{1,0},{2,1},{3,2},{4,7},{5,4},{6,5},{7,6},{8,11},{9,8},{10,9... | collective-permute-start | bytes 294920 | tf_op jit(solution)/shard_map/ppermute | solution.py:40
  61.7 4.5 %collective-permute-start.12 = (bf16[192,256]{1,0:T(8,128)(2,1)S(1)}, bf16[192,256]{1,0:T(8,128)(2,1)S(1)}, u32[]{:S(2)}, u32[]{:S(2)}) collective-permute-start(bf16[192,256]{1,0:T(8,128)(2,1)S(1)} %get-tuple-element.3), channel_id=1, source_target_pairs={{0,28},{4,0},{8,4},{12,8},{16,12},{20,16},{24,20},{28,24},{1,29},{... | collective-permute-start | bytes 294920 | tf_op jit(solution)/shard_map/ppermute | solution.py:29
  61.7 7.2 %collective-permute-start.11 = (bf16[192,256]{1,0:T(8,128)(2,1)S(1)}, bf16[192,256]{1,0:T(8,128)(2,1)S(1)}, u32[]{:S(2)}, u32[]{:S(2)}) collective-permute-start(bf16[192,256]{1,0:T(8,128)(2,1)S(1)} %get-tuple-element.4), channel_id=1, source_target_pairs={{0,24},{4,28},{8,0},{12,4},{16,8},{20,12},{24,16},{28,20},{1,25},{... | collective-permute-start | bytes 294920 | tf_op jit(solution)/shard_map/ppermute | solution.py:29
  63.3 5.7 %collective-permute-start.10 = (bf16[192,256]{1,0:T(8,128)(2,1)S(1)}, bf16[192,256]{1,0:T(8,128)(2,1)S(1)}, u32[]{:S(2)}, u32[]{:S(2)}) collective-permute-start(bf16[192,256]{1,0:T(8,128)(2,1)S(1)} %get-tuple-element.5), channel_id=1, source_target_pairs={{0,20},{4,24},{8,28},{12,0},{16,4},{20,8},{24,12},{28,16},{1,21},{... | collective-permute-start | bytes 294920 | tf_op jit(solution)/shard_map/ppermute | solution.py:29
  64.5 9.9 %collective-permute-start.9 = (bf16[192,256]{1,0:T(8,128)(2,1)S(1)}, bf16[192,256]{1,0:T(8,128)(2,1)S(1)}, u32[]{:S(2)}, u32[]{:S(2)}) collective-permute-start(bf16[192,256]{1,0:T(8,128)(2,1)S(1)} %get-tuple-element.6), channel_id=1, source_target_pairs={{0,16},{4,20},{8,24},{12,28},{16,0},{20,4},{24,8},{28,12},{1,17},{... | collective-permute-start | bytes 294920 | tf_op jit(solution)/shard_map/ppermute | solution.py:29
  65.1 10.0 %collective-permute-start.8 = (bf16[192,256]{1,0:T(8,128)(2,1)S(1)}, bf16[192,256]{1,0:T(8,128)(2,1)S(1)}, u32[]{:S(2)}, u32[]{:S(2)}) collective-permute-start(bf16[192,256]{1,0:T(8,128)(2,1)S(1)} %get-tuple-element.7), channel_id=1, source_target_pairs={{0,12},{4,16},{8,20},{12,24},{16,28},{20,0},{24,4},{28,8},{1,13},{... | collective-permute-start | bytes 294920 | tf_op jit(solution)/shard_map/ppermute | solution.py:29
  66.2 8.8 %collective-permute-start.7 = (bf16[192,256]{1,0:T(8,128)(2,1)S(1)}, bf16[192,256]{1,0:T(8,128)(2,1)S(1)}, u32[]{:S(2)}, u32[]{:S(2)}) collective-permute-start(bf16[192,256]{1,0:T(8,128)(2,1)S(1)} %get-tuple-element.8), channel_id=1, source_target_pairs={{0,8},{4,12},{8,16},{12,20},{16,24},{20,28},{24,0},{28,4},{1,9},{5... | collective-permute-start | bytes 294920 | tf_op jit(solution)/shard_map/ppermute | solution.py:29
  68.9 6.1 %collective-permute-start.6 = (bf16[192,256]{1,0:T(8,128)(2,1)S(1)}, bf16[192,256]{1,0:T(8,128)(2,1)S(1)}, u32[]{:S(2)}, u32[]{:S(2)}) collective-permute-start(bf16[192,256]{1,0:T(8,128)(2,1)S(1)} %get-tuple-element.2), channel_id=1, source_target_pairs={{0,4},{4,8},{8,12},{12,16},{16,20},{20,24},{24,28},{28,0},{1,5},{5... | collective-permute-start | bytes 294920 | tf_op jit(solution)/shard_map/ppermute | solution.py:29
where the time goes:
time: 77.1 us; the launch traced here: 76.7 us
  waiting for transfers between devices  19 us (25%)
  starting transfers between devices  15.5 us (20%)
  local copies, waits for them, and re-layouts  13.1 us (17%)
  matrix products  12.7 us (16%)
  blocking collectives  11.9 us (15%)
  other arithmetic  2.99 us (4%)
  between operations  1.47 us (2%)
    ppermute x10, waiting for transfers between devices, scatter_sum(): got = lax.ppermute(piece, axis, [(i, (i + shift) % n) for i in range(n)])  16.1 us
    all_gather x1, blocking collectives, on_device(): gathered = lax.all_gather(features, 'row', axis=0, tiled=True)  11.9 us
    ppermute x10, starting transfers between devices, scatter_sum(): got = lax.ppermute(piece, axis, [(i, (i + shift) % n) for i in range(n)])  10.6 us
    ppermute x3, starting transfers between devices, gather_rows(): got = lax.ppermute(rows, axis, [(i, (i + shift) % n) for i in range(n)])  4.89 us
    dot_general x1, local copies, waits for them, and re-layouts, on_device(): partial_value = jnp.dot(dense, gathered, preferred_element_type=jnp.float32)  3.62 us
    dot_general x1, matrix products, on_device(): partial_value = jnp.dot(dense, gathered, preferred_element_type=jnp.float32)  3.48 us
    dot_general x1, matrix products, on_device(): lax.dot_general(dense, pulled_block, (((0,), (0,)), ((), ())), preferred_...  2.95 us
    ppermute x3, waiting for transfers between devices, gather_rows(): got = lax.ppermute(rows, axis, [(i, (i + shift) % n) for i in range(n)])  2.94 us
  transfers between devices with their start and end apart: 13, of which 7 were waited for; matrix products, arithmetic and copies ran while one was open for 8% of the time, Pallas kernels for 0%

commit v1 on v0

--- a/solution.py
+++ b/solution.py
@@ -63,7 +63,15 @@
     select = row_hot[:, None, :] * col_hot[None, :, :] * occupied[None, None, :]
     dense = jnp.einsum("tck,kij->ticj", select, blocks, preferred_element_type=jnp.float32)
     dense = dense.astype(jnp.bfloat16).reshape(row_tiles * tile_size, col_tiles * tile_size)
-    gathered = lax.all_gather(features, "row", axis=0, tiled=True)
+    current_block = lax.axis_size("row")
+    x_new = lax.axis_index("row")
+    x_now, h_now, right_arr = (current_block, x_new, features.shape[0])
+    opened, tile_out = (features, 1)
+    while tile_out < x_now:
+        before = lax.ppermute(opened, "row", [(h, (h - tile_out) % x_now) for h in range(x_now)])
+        opened = jnp.concatenate([opened, before], axis=0)
+        tile_out = 2 * tile_out
+    gathered = jnp.roll(opened, h_now * right_arr, axis=0)
     partial_value = jnp.dot(dense, gathered, preferred_element_type=jnp.float32)
     own_sums = scatter_sum(partial_value, "col")
     activated, pulled_own = dense_layer(own_sums, cotangent, weight)

time: 77.1 us -> 82.7 us (1.073)
  blocking collectives: 11.9 us -> 0 us
  starting transfers between devices: 15.5 us -> 22.5 us
  waiting for transfers between devices: 19 us -> 24.5 us
  local copies, waits for them, and re-layouts: 13.1 us -> 17.9 us
  other arithmetic: 2.99 us -> 5.61 us
  matrix products: 12.7 us -> 10.1 us
    all_gather x1 -> x0, blocking collectives: 11.9 us -> none  [on_device(): gathered = lax.all_gather(features, 'row', axis=0, tiled=True)]
    ppermute x0 -> x3, waiting for transfers between devices: none -> 8.84 us  [on_device(): lax.ppermute(opened, 'row', [(h, (h - tile_out) % x_now) for h in range(x...]
    ppermute x0 -> x3, starting transfers between devices: none -> 4.82 us  [on_device(): lax.ppermute(opened, 'row', [(h, (h - tile_out) % x_now) for h in range(x...]
    unnamed x5 -> x16, local copies, waits for them, and re-layouts: 2.23 us -> 7.05 us
    ppermute x10, waiting for transfers between devices: 16.1 us -> 11.4 us  [scatter_sum(): got = lax.ppermute(piece, axis, [(i, (i + shift) % n) for i in range(n)])]
    concatenate x0 -> x2, other arithmetic: none -> 2.62 us  [on_device(): opened = jnp.concatenate([opened, before], axis=0)]
    ppermute x10, starting transfers between devices: 10.6 us -> 13.1 us  [scatter_sum(): got = lax.ppermute(piece, axis, [(i, (i + shift) % n) for i in range(n)])]
    dot_general x1, matrix products: 3.48 us -> 1.7 us  [on_device(): partial_value = jnp.dot(dense, gathered, preferred_element_type=jnp.float32)]
  transfers between devices with their start and end apart: 13 -> 16, of which waited for: 7 -> 12; matrix products, arithmetic and copies ran while one was open for 8% -> 19% of each run, Pallas kernels for 0% -> 0%
where the time goes in v1:
time: 82.7 us; the launch traced here: 82.1 us
  waiting for transfers between devices  24.5 us (30%)
  starting transfers between devices  22.5 us (27%)
  local copies, waits for them, and re-layouts  17.9 us (22%)
  matrix products  10.1 us (12%)
  other arithmetic  5.61 us (7%)
  between operations  1.49 us (2%)
    ppermute x10, starting transfers between devices, scatter_sum(): got = lax.ppermute(piece, axis, [(i, (i + shift) % n) for i in range(n)])  13.1 us
    ppermute x10, waiting for transfers between devices, scatter_sum(): got = lax.ppermute(piece, axis, [(i, (i + shift) % n) for i in range(n)])  11.4 us
    ppermute x3, waiting for transfers between devices, on_device(): lax.ppermute(opened, 'row', [(h, (h - tile_out) % x_now) for h in range(x...  8.84 us
    unnamed x16, local copies, waits for them, and re-layouts  7.05 us
    ppermute x3, starting transfers between devices, on_device(): lax.ppermute(opened, 'row', [(h, (h - tile_out) % x_now) for h in range(x...  4.82 us
    ppermute x3, starting transfers between devices, gather_rows(): got = lax.ppermute(rows, axis, [(i, (i + shift) % n) for i in range(n)])  4.65 us
    ppermute x3, waiting for transfers between devices, gather_rows(): got = lax.ppermute(rows, axis, [(i, (i + shift) % n) for i in range(n)])  4.25 us
    dot_general x1, local copies, waits for them, and re-layouts, on_device(): partial_value = jnp.dot(dense, gathered, preferred_element_type=jnp.float32)  3.62 us
  transfers between devices with their start and end apart: 16, of which 12 were waited for; matrix products, arithmetic and copies ran while one was open for 19% of the time, Pallas kernels for 0%

profile of v1, /device:TPU:0, one launch (start us, length us, event | category | flops | bytes accessed | tf_op | source)
XLA Modules:
  0.0 82.1 jit_solution(14925990449095460570)
XLA Ops:
  0.6 3.4 %collective-permute-start = (bf16[192,256]{1,0:T(8,128)(2,1)}, bf16[192,256]{1,0:T(8,128)(2,1)S(1)}, u32[]{:S(2)}, u32[]{:S(2)}) collective-permute-start(bf16[192,256]{1,0:T(8,128)(2,1)} %param.7), channel_id=1, source_target_pairs={{0,28},{4,0},{8,4},{12,8},{16,12},{20,16},{24,20},{28,24},{1,29},{... | collective-permute-start | bytes 294920 | tf_op jit(solution)/shard_map/ppermute | solution.py:71
  5.4 1.2 %collective-permute-done = bf16[192,256]{1,0:T(8,128)(2,1)S(1)} collective-permute-done((bf16[192,256]{1,0:T(8,128)(2,1)}, bf16[192,256]{1,0:T(8,128)(2,1)S(1)}, u32[]{:S(2)}, u32[]{:S(2)}) %collective-permute-start) | collective-permute-done | bytes 98336 | tf_op jit(solution)/shard_map/ppermute | solution.py:71
  8.8 5.9 %collective-permute-done.1 = bf16[384,256]{1,0:T(8,128)(2,1)S(1)} collective-permute-done((bf16[384,256]{1,0:T(8,128)(2,1)S(1)}, bf16[384,256]{1,0:T(8,128)(2,1)S(1)}, u32[]{:S(2)}, u32[]{:S(2)}) %collective-permute-start.1) | collective-permute-done | bytes 196640 | tf_op jit(solution)/shard_map/ppermute | solution.py:71
  14.7 1.7 %pad_maximum_fusion = bf16[768,256]{1,0:T(8,128)(2,1)} fusion(bf16[384,256]{1,0:T(8,128)(2,1)S(1)} %collective-permute-done.1, bf16[192,256]{1,0:T(8,128)(2,1)S(1)} %collective-permute-done, bf16[192,256]{1,0:T(8,128)(2,1)} %param.7), kind=kLoop, calls=%fused_computation.7 | loop fusion | flops 1179648 | bytes 786432 | tf_op jit(solution)/shard_map/concatenate | solution.py:72
  17.2 2.6 %convolution_convert_fusion = bf16[3,6,256,256]{3,1,2,0:T(8,128)(2,1)S(1)} fusion(bf16[12,256,256]{2,1,0:T(8,128)(2,1)} %bitcast.92, bf16[12]{0:T(256)(128)(2,1)S(1)} %compare_convert_fusion, bf16[6,12]{1,0:T(8,128)(2,1)S(1)} %fusion.22, bf16[3,12]{1,0:T(4,128)(2,1)S(1)} %fusion.26), kind=kOutput, calls=%fused_computation | convolution fusion | flops 29492496 | bytes 3932400 | tf_op jit(solution)/shard_map/tck,kij->ticj/dot_general | solution.py:64
  19.9 3.6 %dot_general.22 = bf16[4,192,1536]{2,1,0:T(8,128)(2,1)} reshape(bf16[3,256,6,256]{3,2,1,0:T(8,128)(2,1)S(1)} %bitcast.88) | data formatting | bytes 4718592 | tf_op jit(solution)/shard_map/dot_general | solution.py:75
  23.5 1.0 %constant_dynamic-update-slice_fusion.7 = bf16[3072,256]{1,0:T(8,128)(2,1)S(1)} fusion(bf16[192,256]{1,0:T(8,128)(2,1)} %param.7), kind=kLoop, calls=%fused_computation.46 | loop fusion | bytes 196608
  25.5 1.7 %collective-permute-done.2 = bf16[768,256]{1,0:T(8,128)(2,1)} collective-permute-done((bf16[768,256]{1,0:T(8,128)(2,1)}, bf16[768,256]{1,0:T(8,128)(2,1)}, u32[]{:S(2)}, u32[]{:S(2)}) %collective-permute-start.2) | collective-permute-done | bytes 393248 | tf_op jit(solution)/shard_map/ppermute | solution.py:71
  27.2 1.0 %constant_dynamic-update-slice_fusion.4 = bf16[3072,256]{1,0:T(8,128)(2,1)S(1)} fusion(bf16[3072,256]{1,0:T(8,128)(2,1)S(1)} %constant_dynamic-update-slice_fusion.5, bf16[768,256]{1,0:T(8,128)(2,1)} %collective-permute-done.2), kind=kLoop, calls=%fused_computation.43 | loop fusion | bytes 786432
  30.0 1.0 %constant_dynamic-update-slice_fusion = bf16[3072,256]{1,0:T(8,128)(2,1)S(1)} fusion(bf16[3072,256]{1,0:T(8,128)(2,1)S(1)} %constant_dynamic-update-slice_fusion.1, bf16[768,256]{1,0:T(8,128)(2,1)} %collective-permute-done.2), kind=kLoop, calls=%fused_computation.39 | loop fusion | bytes 786432 | tf_op jit(solution)/shard_map/jit(_roll_dynamic)/concatenate | solution.py:74
  31.1 1.7 %fusion.28 = (bf16[4,192,256]{2,1,0:T(8,128)(2,1)S(1)}, f32[4,192,256]{2,1,0:T(8,128)}) fusion(bf16[4,192,1536]{2,1,0:T(8,128)(2,1)S(1)} %copy-done.1, bf16[3072,256]{1,0:T(8,128)(2,1)S(1)} %constant_dynamic-update-slice_fusion, s32[]{:T(128)S(6)} %select_n.119), kind=kOutput, calls=%fused_computation.61 | convolution fusion | flops 604176384 | bytes 4325380 | tf_op jit(solution)/shard_map/dot_general | solution.py:75
  33.4 1.6 %collective-permute-start.3 = (bf16[192,256]{1,0:T(8,128)(2,1)}, bf16[192,256]{1,0:T(8,128)(2,1)}, u32[]{:S(2)}, u32[]{:S(2)}) collective-permute-start(bf16[192,256]{1,0:T(8,128)(2,1)} %get-tuple-element.9), channel_id=1, source_target_pairs={{0,1},{1,2},{2,3},{3,0},{4,5},{5,6},{6,7},{7,4},{8,9},{9,10},{10,1... | collective-permute-start | bytes 294920 | tf_op jit(solution)/shard_map/ppermute | solution.py:29
  35.0 2.6 %collective-permute-start.4 = (bf16[192,256]{1,0:T(8,128)(2,1)S(1)}, bf16[192,256]{1,0:T(8,128)(2,1)}, u32[]{:S(2)}, u32[]{:S(2)}) collective-permute-start(bf16[192,256]{1,0:T(8,128)(2,1)S(1)} %get-tuple-element.11), channel_id=1, source_target_pairs={{0,2},{1,3},{2,0},{3,1},{4,6},{5,7},{6,4},{7,5},{8,10},{9,11},{10,... | collective-permute-start | bytes 294920 | tf_op jit(solution)/shard_map/ppermute | solution.py:29
  37.6 1.3 %collective-permute-start.5 = (bf16[192,256]{1,0:T(8,128)(2,1)S(1)}, bf16[192,256]{1,0:T(8,128)(2,1)}, u32[]{:S(2)}, u32[]{:S(2)}) collective-permute-start(bf16[192,256]{1,0:T(8,128)(2,1)S(1)} %get-tuple-element.10), channel_id=1, source_target_pairs={{0,3},{1,0},{2,1},{3,2},{4,7},{5,4},{6,5},{7,6},{8,11},{9,8},{10,9... | collective-permute-start | bytes 294920 | tf_op jit(solution)/shard_map/ppermute | solution.py:29
  39.0 2.2 %collective-permute-done.3 = bf16[192,256]{1,0:T(8,128)(2,1)} collective-permute-done((bf16[192,256]{1,0:T(8,128)(2,1)}, bf16[192,256]{1,0:T(8,128)(2,1)}, u32[]{:S(2)}, u32[]{:S(2)}) %collective-permute-start.3) | collective-permute-done | bytes 98336 | tf_op jit(solution)/shard_map/ppermute | solution.py:29
  41.2 2.4 %collective-permute-done.4 = bf16[192,256]{1,0:T(8,128)(2,1)} collective-permute-done((bf16[192,256]{1,0:T(8,128)(2,1)S(1)}, bf16[192,256]{1,0:T(8,128)(2,1)}, u32[]{:S(2)}, u32[]{:S(2)}) %collective-permute-start.4) | collective-permute-done | bytes 98336 | tf_op jit(solution)/shard_map/ppermute | solution.py:29
  43.6 1.9 %multiply_convert_fusion.1 = (bf16[192,256]{1,0:T(8,128)(2,1)}, f32[192,256]{1,0:T(8,128)S(1)}) fusion(bf16[256,256]{1,0:T(8,128)(2,1)S(1)} %copy-done, bf16[192,256]{1,0:T(8,128)(2,1)} %collective-permute-done.5, bf16[192,256]{1,0:T(8,128)(2,1)} %collective-permute-done.4, bf16[192,256]{1,0:T(8,128)(2,1)} %collective-permute-done.3, ...), kind=kOutput, calls=%fused_computation.22 | convolution fusion | flops 25755648 | bytes 917508 | tf_op jit(solution)/shard_map/dot_general | solution.py:14
  47.2 2.2 %collective-permute-start.6 = (bf16[192,256]{1,0:T(8,128)(2,1)S(1)}, bf16[192,256]{1,0:T(8,128)(2,1)S(1)}, u32[]{:S(2)}, u32[]{:S(2)}) collective-permute-start(bf16[192,256]{1,0:T(8,128)(2,1)S(1)} %get-tuple-element.17), channel_id=1, source_target_pairs={{0,1},{1,2},{2,3},{3,0},{4,5},{5,6},{6,7},{7,4},{8,9},{9,10},{10,1... | collective-permute-start | bytes 294920 | tf_op jit(solution)/shard_map/ppermute | solution.py:40
  49.4 2.2 %copy.16 = bf16[96,8,6,256]{3,1,2,0:T(8,128)(2,1)} copy(bf16[96,8,6,256]{3,2,1,0:T(8,128)(2,1)S(1)} %bitcast.89) | data formatting | bytes 4718592
  51.7 2.8 %copy.14 = bf16[1536,768]{1,0:T(8,128)(2,1)S(1)} copy(bf16[1536,768]{0,1:T(8,128)(2,1)} %bitcast.91) | data formatting | bytes 4718592 | tf_op jit(solution)/shard_map/dot_general | solution.py:79
  54.6 1.7 %collective-permute-start.7 = (bf16[192,256]{1,0:T(8,128)(2,1)S(1)}, bf16[192,256]{1,0:T(8,128)(2,1)S(1)}, u32[]{:S(2)}, u32[]{:S(2)}) collective-permute-start(bf16[192,256]{1,0:T(8,128)(2,1)S(1)} %get-tuple-element.17), channel_id=1, source_target_pairs={{0,2},{1,3},{2,0},{3,1},{4,6},{5,7},{6,4},{7,5},{8,10},{9,11},{10,... | collective-permute-start | bytes 294920 | tf_op jit(solution)/shard_map/ppermute | solution.py:40
  57.6 4.2 %collective-permute-done.7 = bf16[192,256]{1,0:T(8,128)(2,1)S(1)} collective-permute-done((bf16[192,256]{1,0:T(8,128)(2,1)S(1)}, bf16[192,256]{1,0:T(8,128)(2,1)S(1)}, u32[]{:S(2)}, u32[]{:S(2)}) %collective-permute-start.7) | collective-permute-done | bytes 98336 | tf_op jit(solution)/shard_map/ppermute | solution.py:40
  63.2 2.9 %fusion.29 = (bf16[8,192,256]{2,1,0:T(8,128)(2,1)S(1)}, f32[8,192,256]{2,1,0:T(8,128)}) fusion(bf16[8,192,768]{2,1,0:T(8,128)(2,1)S(1)} %bitcast.90, bf16[768,256,1]{1,0,2:T(8,128)(2,1)} %bitcast.20), kind=kOutput, calls=%fused_computation.62 | convolution fusion | flops 604372992 | bytes 5111808 | tf_op jit(solution)/shard_map/dot_general | solution.py:79
  66.2 2.5 %collective-permute-start.10 = (bf16[192,256]{1,0:T(8,128)(2,1)S(1)}, bf16[192,256]{1,0:T(8,128)(2,1)S(1)}, u32[]{:S(2)}, u32[]{:S(2)}) collective-permute-start(bf16[192,256]{1,0:T(8,128)(2,1)S(1)} %get-tuple-element.8), channel_id=1, source_target_pairs={{0,8},{4,12},{8,16},{12,20},{16,24},{20,28},{24,0},{28,4},{1,9},{5... | collective-permute-start | bytes 294920 | tf_op jit(solution)/shard_map/ppermute | solution.py:29
  69.2 1.0 %collective-permute-start.12 = (bf16[192,256]{1,0:T(8,128)(2,1)S(1)}, bf16[192,256]{1,0:T(8,128)(2,1)S(1)}, u32[]{:S(2)}, u32[]{:S(2)}) collective-permute-start(bf16[192,256]{1,0:T(8,128)(2,1)S(1)} %get-tuple-element.6), channel_id=1, source_target_pairs={{0,16},{4,20},{8,24},{12,28},{16,0},{20,4},{24,8},{28,12},{1,17},{... | collective-permute-start | bytes 294920 | tf_op jit(solution)/shard_map/ppermute | solution.py:29
  70.2 1.5 %collective-permute-start.13 = (bf16[192,256]{1,0:T(8,128)(2,1)S(1)}, bf16[192,256]{1,0:T(8,128)(2,1)S(1)}, u32[]{:S(2)}, u32[]{:S(2)}) collective-permute-start(bf16[192,256]{1,0:T(8,128)(2,1)S(1)} %get-tuple-element.5), channel_id=1, source_target_pairs={{0,20},{4,24},{8,28},{12,0},{16,4},{20,8},{24,12},{28,16},{1,21},{... | collective-permute-start | bytes 294920 | tf_op jit(solution)/shard_map/ppermute | solution.py:29
  71.6 1.2 %collective-permute-start.14 = (bf16[192,256]{1,0:T(8,128)(2,1)S(1)}, bf16[192,256]{1,0:T(8,128)(2,1)S(1)}, u32[]{:S(2)}, u32[]{:S(2)}) collective-permute-start(bf16[192,256]{1,0:T(8,128)(2,1)S(1)} %get-tuple-element.4), channel_id=1, source_target_pairs={{0,24},{4,28},{8,0},{12,4},{16,8},{20,12},{24,16},{28,20},{1,25},{... | collective-permute-start | bytes 294920 | tf_op jit(solution)/shard_map/ppermute | solution.py:29
  73.7 1.8 %collective-permute-done.11 = bf16[192,256]{1,0:T(8,128)(2,1)S(1)} collective-permute-done((bf16[192,256]{1,0:T(8,128)(2,1)S(1)}, bf16[192,256]{1,0:T(8,128)(2,1)S(1)}, u32[]{:S(2)}, u32[]{:S(2)}) %collective-permute-start.11) | collective-permute-done | bytes 98336 | tf_op jit(solution)/shard_map/ppermute | solution.py:29
  75.7 1.1 %collective-permute-done.13 = bf16[192,256]{1,0:T(8,128)(2,1)S(1)} collective-permute-done((bf16[192,256]{1,0:T(8,128)(2,1)S(1)}, bf16[192,256]{1,0:T(8,128)(2,1)S(1)}, u32[]{:S(2)}, u32[]{:S(2)}) %collective-permute-start.13) | collective-permute-done | bytes 98336 | tf_op jit(solution)/shard_map/ppermute | solution.py:29
  77.1 1.0 %collective-permute-done.15 = bf16[192,256]{1,0:T(8,128)(2,1)S(1)} collective-permute-done((bf16[192,256]{1,0:T(8,128)(2,1)S(1)}, bf16[192,256]{1,0:T(8,128)(2,1)S(1)}, u32[]{:S(2)}, u32[]{:S(2)}) %collective-permute-start.15) | collective-permute-done | bytes 98336 | tf_op jit(solution)/shard_map/ppermute | solution.py:29
  78.2 2.3 %collective-permute-done.9 = bf16[192,256]{1,0:T(8,128)(2,1)S(1)} collective-permute-done((bf16[192,256]{1,0:T(8,128)(2,1)S(1)}, bf16[192,256]{1,0:T(8,128)(2,1)S(1)}, u32[]{:S(2)}, u32[]{:S(2)}) %collective-permute-start.9) | collective-permute-done | bytes 98336 | tf_op jit(solution)/shard_map/ppermute | solution.py:29
  80.5 1.7 %fusion.11 = bf16[192,256]{1,0:T(8,128)(2,1)} fusion(bf16[192,256]{1,0:T(8,128)(2,1)S(1)} %collective-permute-done.15, bf16[192,256]{1,0:T(8,128)(2,1)S(1)} %collective-permute-done.14, bf16[192,256]{1,0:T(8,128)(2,1)S(1)} %collective-permute-done.13, bf16[192,256]{1,0:T(8,128)(2,1)S(1)} %collective-permute-done.12, ...), kind=kLoop, calls=%fused_computation.16 | loop fusion | flops 737280 | bytes 983044 | tf_op jit(solution)/shard_map/convert_element_type | solution.py:82
  (36 shorter events, 13.4 us)
Async XLA Ops:
  0.6 43.0 %copy-start = (bf16[256,256]{1,0:T(8,128)(2,1)S(1)}, bf16[256,256]{1,0:T(8,128)(2,1)}, u32[]{:S(2)}) copy-start(bf16[256,256]{1,0:T(8,128)(2,1)} %param.12) | copy-start | bytes 393220
  0.6 5.9 %collective-permute-start = (bf16[192,256]{1,0:T(8,128)(2,1)}, bf16[192,256]{1,0:T(8,128)(2,1)S(1)}, u32[]{:S(2)}, u32[]{:S(2)}) collective-permute-start(bf16[192,256]{1,0:T(8,128)(2,1)} %param.7), channel_id=1, source_target_pairs={{0,28},{4,0},{8,4},{12,8},{16,12},{20,16},{24,20},{28,24},{1,29},{... | collective-permute-start | bytes 294920 | tf_op jit(solution)/shard_map/ppermute | solution.py:71
  6.6 10.6 %copy-start.2 = (bf16[192,256]{1,0:T(8,128)(2,1)}, bf16[192,256]{1,0:T(8,128)(2,1)S(1)}, u32[]{:S(2)}) copy-start(bf16[192,256]{1,0:T(8,128)(2,1)S(1)} %collective-permute-done) | copy-start | bytes 294916
  7.5 7.2 %collective-permute-start.1 = (bf16[384,256]{1,0:T(8,128)(2,1)S(1)}, bf16[384,256]{1,0:T(8,128)(2,1)S(1)}, u32[]{:S(2)}, u32[]{:S(2)}) collective-permute-start(bf16[384,256]{1,0:T(8,128)(2,1)S(1)} %pad_maximum_fusion.1), channel_id=1, source_target_pairs={{0,24},{4,28},{8,0},{12,4},{16,8},{20,12},{24,16},{28,20},{1,25},{... | collective-permute-start | bytes 589832 | tf_op jit(solution)/shard_map/ppermute | solution.py:71
  16.4 10.8 %collective-permute-start.2 = (bf16[768,256]{1,0:T(8,128)(2,1)}, bf16[768,256]{1,0:T(8,128)(2,1)}, u32[]{:S(2)}, u32[]{:S(2)}) collective-permute-start(bf16[768,256]{1,0:T(8,128)(2,1)} %pad_maximum_fusion), channel_id=1, source_target_pairs={{0,16},{4,20},{8,24},{12,28},{16,0},{20,4},{24,8},{28,12},{1,17},{... | collective-permute-start | bytes 1179656 | tf_op jit(solution)/shard_map/ppermute | solution.py:71
  23.5 7.6 %copy-start.1 = (bf16[4,192,1536]{2,1,0:T(8,128)(2,1)S(1)}, bf16[4,192,1536]{2,1,0:T(8,128)(2,1)}, u32[]{:S(2)}) copy-start(bf16[4,192,1536]{2,1,0:T(8,128)(2,1)} %dot_general.22) | copy-start | bytes 7077892
  33.4 7.7 %collective-permute-start.3 = (bf16[192,256]{1,0:T(8,128)(2,1)}, bf16[192,256]{1,0:T(8,128)(2,1)}, u32[]{:S(2)}, u32[]{:S(2)}) collective-permute-start(bf16[192,256]{1,0:T(8,128)(2,1)} %get-tuple-element.9), channel_id=1, source_target_pairs={{0,1},{1,2},{2,3},{3,0},{4,5},{5,6},{6,7},{7,4},{8,9},{9,10},{10,1... | collective-permute-start | bytes 294920 | tf_op jit(solution)/shard_map/ppermute | solution.py:29
  35.0 8.6 %collective-permute-start.4 = (bf16[192,256]{1,0:T(8,128)(2,1)S(1)}, bf16[192,256]{1,0:T(8,128)(2,1)}, u32[]{:S(2)}, u32[]{:S(2)}) collective-permute-start(bf16[192,256]{1,0:T(8,128)(2,1)S(1)} %get-tuple-element.11), channel_id=1, source_target_pairs={{0,2},{1,3},{2,0},{3,1},{4,6},{5,7},{6,4},{7,5},{8,10},{9,11},{10,... | collective-permute-start | bytes 294920 | tf_op jit(solution)/shard_map/ppermute | solution.py:29
  37.6 6.0 %collective-permute-start.5 = (bf16[192,256]{1,0:T(8,128)(2,1)S(1)}, bf16[192,256]{1,0:T(8,128)(2,1)}, u32[]{:S(2)}, u32[]{:S(2)}) collective-permute-start(bf16[192,256]{1,0:T(8,128)(2,1)S(1)} %get-tuple-element.10), channel_id=1, source_target_pairs={{0,3},{1,0},{2,1},{3,2},{4,7},{5,4},{6,5},{7,6},{8,11},{9,8},{10,9... | collective-permute-start | bytes 294920 | tf_op jit(solution)/shard_map/ppermute | solution.py:29
  38.9 7.4 %copy-start.3 = (bf16[192,256]{1,0:T(8,128)(2,1)S(1)}, bf16[192,256]{1,0:T(8,128)(2,1)}, u32[]{:S(2)}) copy-start(bf16[192,256]{1,0:T(8,128)(2,1)} %param.13) | copy-start | bytes 294916
  47.2 9.8 %collective-permute-start.6 = (bf16[192,256]{1,0:T(8,128)(2,1)S(1)}, bf16[192,256]{1,0:T(8,128)(2,1)S(1)}, u32[]{:S(2)}, u32[]{:S(2)}) collective-permute-start(bf16[192,256]{1,0:T(8,128)(2,1)S(1)} %get-tuple-element.17), channel_id=1, source_target_pairs={{0,1},{1,2},{2,3},{3,0},{4,5},{5,6},{6,7},{7,4},{8,9},{9,10},{10,1... | collective-permute-start | bytes 294920 | tf_op jit(solution)/shard_map/ppermute | solution.py:40
  54.6 7.3 %collective-permute-start.7 = (bf16[192,256]{1,0:T(8,128)(2,1)S(1)}, bf16[192,256]{1,0:T(8,128)(2,1)S(1)}, u32[]{:S(2)}, u32[]{:S(2)}) collective-permute-start(bf16[192,256]{1,0:T(8,128)(2,1)S(1)} %get-tuple-element.17), channel_id=1, source_target_pairs={{0,2},{1,3},{2,0},{3,1},{4,6},{5,7},{6,4},{7,5},{8,10},{9,11},{10,... | collective-permute-start | bytes 294920 | tf_op jit(solution)/shard_map/ppermute | solution.py:40
  56.2 6.3 %collective-permute-start.8 = (bf16[192,256]{1,0:T(8,128)(2,1)S(1)}, bf16[192,256]{1,0:T(8,128)(2,1)S(1)}, u32[]{:S(2)}, u32[]{:S(2)}) collective-permute-start(bf16[192,256]{1,0:T(8,128)(2,1)S(1)} %get-tuple-element.17), channel_id=1, source_target_pairs={{0,3},{1,0},{2,1},{3,2},{4,7},{5,4},{6,5},{7,6},{8,11},{9,8},{10,9... | collective-permute-start | bytes 294920 | tf_op jit(solution)/shard_map/ppermute | solution.py:40
  66.2 6.7 %collective-permute-start.10 = (bf16[192,256]{1,0:T(8,128)(2,1)S(1)}, bf16[192,256]{1,0:T(8,128)(2,1)S(1)}, u32[]{:S(2)}, u32[]{:S(2)}) collective-permute-start(bf16[192,256]{1,0:T(8,128)(2,1)S(1)} %get-tuple-element.8), channel_id=1, source_target_pairs={{0,8},{4,12},{8,16},{12,20},{16,24},{20,28},{24,0},{28,4},{1,9},{5... | collective-permute-start | bytes 294920 | tf_op jit(solution)/shard_map/ppermute | solution.py:29
  68.6 6.9 %collective-permute-start.11 = (bf16[192,256]{1,0:T(8,128)(2,1)S(1)}, bf16[192,256]{1,0:T(8,128)(2,1)S(1)}, u32[]{:S(2)}, u32[]{:S(2)}) collective-permute-start(bf16[192,256]{1,0:T(8,128)(2,1)S(1)} %get-tuple-element.7), channel_id=1, source_target_pairs={{0,12},{4,16},{8,20},{12,24},{16,28},{20,0},{24,4},{28,8},{1,13},{... | collective-permute-start | bytes 294920 | tf_op jit(solution)/shard_map/ppermute | solution.py:29
  69.2 6.5 %collective-permute-start.12 = (bf16[192,256]{1,0:T(8,128)(2,1)S(1)}, bf16[192,256]{1,0:T(8,128)(2,1)S(1)}, u32[]{:S(2)}, u32[]{:S(2)}) collective-permute-start(bf16[192,256]{1,0:T(8,128)(2,1)S(1)} %get-tuple-element.6), channel_id=1, source_target_pairs={{0,16},{4,20},{8,24},{12,28},{16,0},{20,4},{24,8},{28,12},{1,17},{... | collective-permute-start | bytes 294920 | tf_op jit(solution)/shard_map/ppermute | solution.py:29
  70.2 6.6 %collective-permute-start.13 = (bf16[192,256]{1,0:T(8,128)(2,1)S(1)}, bf16[192,256]{1,0:T(8,128)(2,1)S(1)}, u32[]{:S(2)}, u32[]{:S(2)}) collective-permute-start(bf16[192,256]{1,0:T(8,128)(2,1)S(1)} %get-tuple-element.5), channel_id=1, source_target_pairs={{0,20},{4,24},{8,28},{12,0},{16,4},{20,8},{24,12},{28,16},{1,21},{... | collective-permute-start | bytes 294920 | tf_op jit(solution)/shard_map/ppermute | solution.py:29
  71.6 5.5 %collective-permute-start.14 = (bf16[192,256]{1,0:T(8,128)(2,1)S(1)}, bf16[192,256]{1,0:T(8,128)(2,1)S(1)}, u32[]{:S(2)}, u32[]{:S(2)}) collective-permute-start(bf16[192,256]{1,0:T(8,128)(2,1)S(1)} %get-tuple-element.4), channel_id=1, source_target_pairs={{0,24},{4,28},{8,0},{12,4},{16,8},{20,12},{24,16},{28,20},{1,25},{... | collective-permute-start | bytes 294920 | tf_op jit(solution)/shard_map/ppermute | solution.py:29
  72.9 5.3 %collective-permute-start.15 = (bf16[192,256]{1,0:T(8,128)(2,1)S(1)}, bf16[192,256]{1,0:T(8,128)(2,1)S(1)}, u32[]{:S(2)}, u32[]{:S(2)}) collective-permute-start(bf16[192,256]{1,0:T(8,128)(2,1)S(1)} %get-tuple-element.3), channel_id=1, source_target_pairs={{0,28},{4,0},{8,4},{12,8},{16,12},{20,16},{24,20},{28,24},{1,29},{... | collective-permute-start | bytes 294920 | tf_op jit(solution)/shard_map/ppermute | solution.py:29
  75.5 4.9 %collective-permute-start.9 = (bf16[192,256]{1,0:T(8,128)(2,1)S(1)}, bf16[192,256]{1,0:T(8,128)(2,1)S(1)}, u32[]{:S(2)}, u32[]{:S(2)}) collective-permute-start(bf16[192,256]{1,0:T(8,128)(2,1)S(1)} %get-tuple-element.2), channel_id=1, source_target_pairs={{0,4},{4,8},{8,12},{12,16},{16,20},{20,24},{24,28},{28,0},{1,5},{5... | collective-permute-start | bytes 294920 | tf_op jit(solution)/shard_map/ppermute | solution.py:29
